TPU v7x, 32 devices: a whole 2x2x4 slice. The times are simulated.
32 devices in a mesh: blk: 8 (over y, x, core), slab: 4 (over z).
Axes of the slice: x: 2, y: 2, z: 4, core: 2. Of those that a mesh axis runs over, the one named last changes fastest.
Arguments:
- queries: bfloat16 [4096, 4096], P(('blk', 'slab')), may hold values from -8 to 8
- passages: bfloat16 [2816, 4096], P(('blk', 'slab')), may hold values from -6 to 6
- positive: int32 [4096], P(('blk', 'slab')), may hold values from 0 to 703
- hard_ids: int32 [4096, 8], P(('blk', 'slab')), may hold values from 0 to 2815, as said below
Outputs:
- query_loss: float32 [4096], P(('blk', 'slab'))
- query_grad: float32 [4096, 4096], P(('blk', 'slab'))
- passage_grad: float32 [2816, 4096], P(('blk', 'slab'))
Inputs may be any that keep to these rules, and one draw needn't show every extreme that they name: `hard_ids`: passage row f * 88 + t lies on the device of flat index f = b * 4 + s. Of the hard-negative ids of the 128 queries of one device, at most 36 name rows that lie on any one device, and in every draw some device has exactly 36 ids on some one device.
All inputs are finite; a program needn't handle non-finite values.
Results may differ from a plain program's by a relative error of at most 0.008.
Values may be sent and summed in bfloat16 or wider, within the bound.
No kernel may reach another device: no remote copies, remote signals or barrier semaphores. Data moves between devices by JAX's collectives and lax.ppermute only.
A program may use at most 192 MiB of HBM per device.

v0:
```python
import math
import jax
import jax.numpy as jnp
from jax import lax
from jax.sharding import PartitionSpec as P


def per_device(queries, passages, positive, hard_ids):
    slabs = lax.axis_size("slab")
    my_slab = lax.axis_index("slab")
    query_rows_dev, model_width = queries.shape
    passage_rows_dev = passages.shape[0]
    hard_count = hard_ids.shape[1]
    logit_scale = 3.0 / math.sqrt(model_width)
    contract_rows = (((1,), (1,)), ((), ()))
    contract_cols = (((0,), (0,)), ((), ()))
    pool = lax.all_gather(passages, "blk", axis=0, tiled=True)
    pool_size = pool.shape[0]
    column_queries = lax.all_gather(queries, "slab", axis=0, tiled=True)
    column_ids = lax.all_gather(hard_ids, "slab", axis=0, tiled=True)
    column_rows = column_queries.shape[0]
    scores = (
        lax.dot_general(column_queries, pool, contract_rows, preferred_element_type=jnp.float32)
        * logit_scale
    )
    own_start = my_slab * query_rows_dev
    pooled = lax.dynamic_slice_in_dim(scores, own_start, query_rows_dev, axis=0)
    owner_dev = column_ids // passage_rows_dev
    owner_slab = owner_dev % slabs
    hard_pos = owner_dev // slabs * passage_rows_dev + column_ids % passage_rows_dev
    mine = owner_slab == my_slab
    hard_mine = jnp.where(mine, jnp.take_along_axis(scores, hard_pos, axis=1), 0.0)
    pool_max = jnp.max(pooled, axis=1)
    pool_sum = jnp.sum(jnp.exp(pooled - pool_max[:, None]), axis=1)
    payload = jnp.concatenate([hard_mine.reshape(-1), pool_max, pool_sum])
    gathered = lax.all_gather(payload, "slab", axis=0)
    hard_split = column_rows * hard_count
    hard_all = jnp.take_along_axis(
        gathered[:, :hard_split].reshape(slabs, column_rows, hard_count), owner_slab[None], axis=0
    )[0]
    stats = gathered[:, hard_split:].reshape(slabs, 2, query_rows_dev)
    max_all = stats[:, 0].reshape(column_rows)
    sum_all = stats[:, 1].reshape(column_rows)
    row_top = jnp.maximum(max_all, jnp.max(hard_all, axis=1))
    row_total = sum_all * jnp.exp(max_all - row_top) + jnp.sum(
        jnp.exp(hard_all - row_top[:, None]), axis=1
    )
    lse_all = row_top + jnp.log(row_total)
    row_lse = lax.dynamic_slice_in_dim(lse_all, own_start, query_rows_dev)
    onehot = (jnp.arange(pool_size, dtype=jnp.int32)[None, :] == positive[:, None]).astype(
        jnp.float32
    )
    query_loss = row_lse - jnp.sum(onehot * pooled, axis=1)
    coef_pool = (jnp.exp(pooled - row_lse[:, None]) - onehot).astype(jnp.bfloat16)
    coef_hard = jnp.where(
        mine,
        jnp.exp(hard_mine - lse_all[:, None]).astype(jnp.bfloat16),
        jnp.zeros((), jnp.bfloat16),
    )
    hard_matrix = jnp.sum(
        jnp.where(
            hard_pos[:, :, None] == jnp.arange(pool_size, dtype=jnp.int32)[None, None, :],
            coef_hard.astype(jnp.float32)[:, :, None],
            0.0,
        ),
        axis=1,
    ).astype(jnp.bfloat16)
    hard_grad = jnp.dot(hard_matrix, pool, preferred_element_type=jnp.float32).astype(jnp.bfloat16)
    hard_grad = lax.psum_scatter(hard_grad, "slab", scatter_dimension=0, tiled=True)
    pool_grad = jnp.dot(coef_pool, pool, preferred_element_type=jnp.float32)
    query_grad = pool_grad + hard_grad.astype(jnp.float32)
    partial = lax.dot_general(
        coef_pool, queries, contract_cols, preferred_element_type=jnp.float32
    ) + lax.dot_general(
        hard_matrix, column_queries, contract_cols, preferred_element_type=jnp.float32
    )
    passage_grad = lax.psum_scatter(
        partial.astype(jnp.bfloat16), "blk", scatter_dimension=0, tiled=True
    ).astype(jnp.float32)
    return (query_loss, query_grad, passage_grad)


def solution(mesh):
    return jax.shard_map(
        per_device,
        mesh=mesh,
        in_specs=(
            P(("blk", "slab"), None),
            P(("blk", "slab"), None),
            P(("blk", "slab")),
            P(("blk", "slab"), None),
        ),
        out_specs=(P(("blk", "slab")), P(("blk", "slab"), None), P(("blk", "slab"), None)),
        check_vma=False,
    )
```

profile of v0, /device:TPU:0, one launch (start us, length us, event | category | flops | bytes accessed | tf_op | source)
XLA Modules:
  0.0 382.8 jit_solution(10937758230135534292)
XLA Ops:
  7.2 0.7 all-gather.5.cloned.1.call-update
  7.9 0.7 all-gather.7.cloned.1.call-update
  8.7 14.9 %all_gather.15 = s32[512,8]{0,1:T(8,128)S(1)} all-gather(s32[128,8]{0,1:T(8,128)} %param.7), channel_id=1, replica_groups=mesh['blk'=8,'slab'=4] {'slab'}, dimensions={0}, use_global_device_ids=true | all-gather | bytes 20480 | tf_op jit(solution)/shard_map/all_gather | solution.py:20
  23.9 0.2 reshape.91
  24.3 68.7 %all-gather.5.cloned.1.call-done = bf16[512,4096]{1,0:T(8,128)(2,1)} async-done(((bf16[128,4096]{1,0:T(8,128)(2,1)}), bf16[512,4096]{1,0:T(8,128)(2,1)}) %all-gather.5.cloned.1.call-update) | async-done | bytes 4194320 | tf_op jit(solution)/shard_map/all_gather | solution.py:19
  93.1 43.8 %all-gather.7.cloned.1.call-done = bf16[704,4096]{1,0:T(8,128)(2,1)} async-done(((bf16[88,4096]{1,0:T(8,128)(2,1)}), bf16[704,4096]{1,0:T(8,128)(2,1)}) %all-gather.7.cloned.1.call-update) | async-done | bytes 5767184 | tf_op jit(solution)/shard_map/all_gather | solution.py:17
  136.8 6.5 %convolution_multiply_fusion = f32[512,704]{0,1:T(8,128)S(1)} fusion(bf16[512,4096]{1,0:T(8,128)(2,1)} %all-gather.5.cloned.1.call-done, bf16[704,4096]{1,0:T(8,128)(2,1)} %all-gather.7.cloned.1.call-done), kind=kOutput, calls=%fused_computation.7 | convolution fusion | flops 2953150464 | bytes 11403264 | tf_op jit(solution)/shard_map/dot_general | solution.py:23
  143.3 33.0 %gather_fusion = f32[4096]{0:T(1024)S(1)} fusion(f32[512,704]{0,1:T(8,128)S(1)} %convolution_multiply_fusion, s32[4096]{0:T(1024)S(1)} %reshape.83), kind=kCustom, calls=%fused_computation | custom fusion | bytes 65536 | tf_op jit(solution)/shard_map/jit(take_along_axis)/gather | solution.py:32
  176.5 0.2 reshape.86
  176.9 0.2 reshape.79
  177.2 13.3 %all-gather.1 = f32[4,1,4352]{2,1,0:T(1,128)S(1)} all-gather(f32[1,1,4352]{2,1,0:T(1,128)S(1)} %reshape.105), channel_id=2, replica_groups=mesh['blk'=8,'slab'=4] {'slab'}, dimensions={0}, use_global_device_ids=true | all-gather | bytes 87040 | tf_op jit(solution)/shard_map/all_gather | solution.py:36
  190.5 0.6 reshape.81
  191.1 33.1 %gather_fusion.1 = f32[4096]{0:T(1024)S(1)} fusion(f32[4,512,8]{2,1,0:T(8,128)S(1)} %reshape.81, s32[4096]{0:T(1024)S(1)} %reshape.91), kind=kCustom, calls=%fused_computation.1 | custom fusion | bytes 81920 | tf_op jit(solution)/shard_map/jit(take_along_axis)/gather | solution.py:38
  224.3 0.2 gather.12
  224.6 1.5 select_reduce_fusion
  226.1 7.6 %convolution_convert_fusion = bf16[512,4096]{1,0:T(8,128)(2,1)} fusion(bf16[704,4096]{1,0:T(8,128)(2,1)} %all-gather.7.cloned.1.call-done, bf16[512,704]{0,1:T(8,128)(2,1)S(1)} %select_reduce_fusion), kind=kOutput, calls=%fused_computation.5 | convolution fusion | flops 2954887168 | bytes 10682368 | tf_op jit(solution)/shard_map/dot_general | solution.py:68
  233.8 0.2 reduce-scatter.5.cloned.1.call-start
  234.0 0.6 fusion.17
  234.6 5.1 %fusion.20 = f32[704,4096]{1,0:T(8,128)S(1)} fusion(bf16[512,704]{0,1:T(8,128)(2,1)S(1)} %select_reduce_fusion, bf16[512,4096]{1,0:T(8,128)(2,1)} %all-gather.5.cloned.1.call-done), kind=kOutput, calls=%fused_computation.57 | convolution fusion | flops 2952790016 | bytes 16449536 | tf_op jit(solution)/shard_map/dot_general | solution.py:74
  239.7 4.2 %add_convert_fusion = bf16[704,4096]{1,0:T(8,128)(2,1)} fusion(f32[704,4096]{1,0:T(8,128)S(1)} %fusion.20, bf16[128,4096]{1,0:T(8,128)(2,1)S(1)} %copy-done, f32[512,704]{0,1:T(8,128)S(1)} %convolution_multiply_fusion, s32[]{:T(128)S(6)} %select_n.62, f32[128]{0:T(128)S(1)} %get-tuple-element.6, s32[128]{0:T(128)S(1)} %copy-done.1), kind=kOutput, calls=%fused_computation.2 | convolution fusion | flops 744415232 | bytes 18711556 | tf_op jit(solution)/shard_map/dot_general | solution.py:72
  244.0 66.7 %reduce-scatter.3.cloned.1.call-done = bf16[128,4096]{1,0:T(8,128)(2,1)} async-done(((bf16[512,4096]{1,0:T(8,128)(2,1)}), bf16[128,4096]{1,0:T(8,128)(2,1)}) %reduce-scatter.3.cloned.1.call-update) | async-done | bytes 1048592 | tf_op jit(solution)/shard_map/reduce_scatter | solution.py:69
  310.6 5.3 %convolution_add_fusion = f32[128,4096]{1,0:T(8,128)} fusion(bf16[704,4096]{1,0:T(8,128)(2,1)} %all-gather.7.cloned.1.call-done, bf16[128,4096]{1,0:T(8,128)(2,1)} %reduce-scatter.3.cloned.1.call-done, f32[512,704]{0,1:T(8,128)S(1)} %convolution_multiply_fusion, s32[]{:T(128)S(6)} %select_n.62, f32[128]{0:T(128)S(1)} %get-tuple-element.6, s32[128]{0:T(128)S(1)} %copy-done.1), kind=kOutput, calls=%fused_computation.6 | convolution fusion | flops 739696640 | bytes 9274372 | tf_op jit(solution)/shard_map/dot_general | solution.py:70
  315.9 58.0 %reduce-scatter.5.cloned.1.call-done = bf16[88,4096]{1,0:T(8,128)(2,1)} async-done(((bf16[704,4096]{1,0:T(8,128)(2,1)}), bf16[88,4096]{1,0:T(8,128)(2,1)}) %reduce-scatter.5.cloned.1.call-update) | async-done | bytes 720912 | tf_op jit(solution)/shard_map/reduce_scatter | solution.py:77
  373.9 2.3 convert_element_type.35
  (36 shorter events, 1.4 us)
Async XLA Ops:
  7.2 85.9 %all-gather.5.cloned.1.call-start = ((), (), s32[]{:S(2)}) async-start(), calls=%async_computation.2 | async-start | bytes 5242880 | tf_op jit(solution)/shard_map/all_gather | solution.py:19
  7.9 128.9 %all-gather.7.cloned.1.call-start = ((), (), s32[]{:S(2)}) async-start(), calls=%async_computation.3 | async-start | bytes 6488064 | tf_op jit(solution)/shard_map/all_gather | solution.py:17
  8.6 302.0 %reduce-scatter.3.cloned.1.call-start = ((), (), s32[]{:S(2)}) async-start(), calls=%async_computation.4 | async-start | bytes 5242880 | tf_op jit(solution)/shard_map/reduce_scatter | solution.py:69
  143.3 33.7 %copy-start.1 = (s32[128]{0:T(128)S(1)}, s32[128]{0:T(128)}, u32[]{:S(2)}) copy-start(s32[128]{0:T(128)} %param.6) | copy-start | bytes 1540
  233.8 140.1 %reduce-scatter.5.cloned.1.call-start = ((), (), s32[]{:S(2)}) async-start(), calls=%async_computation.5 | async-start | bytes 6488064 | tf_op jit(solution)/shard_map/reduce_scatter | solution.py:77
  234.6 5.1 %copy-start = (bf16[128,4096]{1,0:T(8,128)(2,1)S(1)}, bf16[128,4096]{1,0:T(8,128)(2,1)}, u32[]{:S(2)}) copy-start(bf16[128,4096]{1,0:T(8,128)(2,1)} %param.4) | copy-start | bytes 3145732
Sparse Core Ops, SparseCore 0:
  9.6 83.4 all-gather.4
  94.9 41.8 all-gather.6
  233.9 76.6 reduce-scatter.2
  314.3 59.5 reduce-scatter.4
where the time goes:
time: 383 us
  waiting for transfers between devices  239 us (62%)
  local copies, waits for them, and re-layouts  68.1 us (18%)
  matrix products  28.7 us (7%)
  blocking collectives  28.2 us (7%)
  between operations  14 us (4%)
  other arithmetic  4.86 us (1%)
    all_gather x1, waiting for transfers between devices, per_device(): column_queries = lax.all_gather(queries, 'slab', axis=0, tiled=True)  68.7 us
    reduce_scatter x1, waiting for transfers between devices, per_device(): lax.psum_scatter(hard_grad, 'slab', scatter_dimension=0, tiled=True)  66.7 us
    reduce_scatter x1, waiting for transfers between devices, per_device(): lax.psum_scatter(partial.astype(jnp.bfloat16), 'blk', scatter_dimension=0...  58 us
    all_gather x1, waiting for transfers between devices, per_device(): pool = lax.all_gather(passages, 'blk', axis=0, tiled=True)  43.8 us
    gather x5, local copies, waits for them, and re-layouts, per_device(): jnp.take_along_axis(gathered[:, :hard_split].reshape(slabs, column_rows,...  33.6 us
    gather x5, local copies, waits for them, and re-layouts, per_device(): jnp.take_along_axis(scores, hard_pos, axis=1)  33.6 us
    all_gather x1, blocking collectives, per_device(): column_ids = lax.all_gather(hard_ids, 'slab', axis=0, tiled=True)  14.9 us
    all_gather x1, blocking collectives, per_device(): gathered = lax.all_gather(payload, 'slab', axis=0)  13.3 us
  transfers between devices with their start and end apart: 4, of which 4 were waited for; matrix products, arithmetic and copies ran while one was open for 4% of the time, Pallas kernels for 0%

commit v1 on v0

--- a/solution.py
+++ b/solution.py
@@ -16,7 +16,29 @@
     contract_cols = (((0,), (0,)), ((), ()))
     pool = lax.all_gather(passages, "blk", axis=0, tiled=True)
     pool_size = pool.shape[0]
-    column_queries = lax.all_gather(queries, "slab", axis=0, tiled=True)
+    wide_out = lax.axis_size("slab")
+    far_arr = lax.axis_index("slab")
+    before, left_arr, piece_next = (wide_out, far_arr, queries.shape[0])
+    items = [(i0, (i0 + 1) % before) for i0 in range(before)]
+    panels = [(i0, (i0 - 1) % before) for i0 in range(before)]
+    column_queries = jnp.zeros(
+        (*queries.shape[:0], before * piece_next, *queries.shape[1:]), queries.dtype
+    )
+    column_queries = lax.dynamic_update_slice_in_dim(
+        column_queries, queries, left_arr * piece_next, axis=0
+    )
+    near = last = queries
+    big = before // 2
+    for rr in range(1, big + 1):
+        near = lax.ppermute(near, "slab", items)
+        column_queries = lax.dynamic_update_slice_in_dim(
+            column_queries, near, (left_arr - rr) % before * piece_next, axis=0
+        )
+        if rr < before - big:
+            last = lax.ppermute(last, "slab", panels)
+            column_queries = lax.dynamic_update_slice_in_dim(
+                column_queries, last, (left_arr + rr) % before * piece_next, axis=0
+            )
     column_ids = lax.all_gather(hard_ids, "slab", axis=0, tiled=True)
     column_rows = column_queries.shape[0]
     scores = (

time: 383 us -> 339 us (0.89)
  waiting for transfers between devices: 239 us -> 145 us
  blocking collectives: 28.2 us -> 66.1 us
  local copies, waits for them, and re-layouts: 68.1 us -> 76.2 us
  starting transfers between devices: 0.34 us -> 5.53 us
    all_gather x1 -> x0, waiting for transfers between devices: 68.7 us -> none  [per_device(): column_queries = lax.all_gather(queries, 'slab', axis=0, tiled=True)]
    all_gather x1, waiting for transfers between devices: 43.8 us -> 0.01 us  [per_device(): pool = lax.all_gather(passages, 'blk', axis=0, tiled=True)]
    all_gather x1, blocking collectives: 14.9 us -> 53 us  [per_device(): column_ids = lax.all_gather(hard_ids, 'slab', axis=0, tiled=True)]
    ppermute x0 -> x3, waiting for transfers between devices: none -> 20 us  [the longest x2 20 us: per_device(): near = lax.ppermute(near, 'slab', items)]
    ppermute x0 -> x3, starting transfers between devices: none -> 5.23 us  [the longest x2 3.13 us: per_device(): near = lax.ppermute(near, 'slab', items)]
    dynamic_update_slice x0 -> x4, local copies, waits for them, and re-layouts: none -> 4.64 us  [the longest x1 2.28 us: per_device(): lax.dynamic_update_slice_in_dim(column_queries, last, (left_arr + rr) % b...]
  transfers between devices with their start and end apart: 4 -> 6, of which waited for: 4 -> 3; matrix products, arithmetic and copies ran while one was open for 4% -> 5% of each run, Pallas kernels for 0% -> 0%
where the time goes in v1:
time: 339 us; the launch traced here: 338 us
  waiting for transfers between devices  145 us (43%)
  local copies, waits for them, and re-layouts  76.2 us (22%)
  blocking collectives  66.1 us (19%)
  matrix products  26 us (8%)
  between operations  14.1 us (4%)
  starting transfers between devices  5.53 us (2%)
  other arithmetic  4.86 us (1%)
    reduce_scatter x1, waiting for transfers between devices, per_device(): lax.psum_scatter(hard_grad, 'slab', scatter_dimension=0, tiled=True)  66.5 us
    reduce_scatter x1, waiting for transfers between devices, per_device(): lax.psum_scatter(partial.astype(jnp.bfloat16), 'blk', scatter_dimension=0...  58.1 us
    all_gather x1, blocking collectives, per_device(): column_ids = lax.all_gather(hard_ids, 'slab', axis=0, tiled=True)  53 us
    gather x5, local copies, waits for them, and re-layouts, per_device(): jnp.take_along_axis(gathered[:, :hard_split].reshape(slabs, column_rows,...  33.6 us
    gather x5, local copies, waits for them, and re-layouts, per_device(): jnp.take_along_axis(scores, hard_pos, axis=1)  33.6 us
    ppermute x2, waiting for transfers between devices, per_device(): near = lax.ppermute(near, 'slab', items)  20 us
    all_gather x1, blocking collectives, per_device(): gathered = lax.all_gather(payload, 'slab', axis=0)  13.2 us
    dot_general x1, matrix products, per_device(): jnp.dot(hard_matrix, pool, preferred_element_type=jnp.float32)  7.64 us
  transfers between devices with their start and end apart: 6, of which 3 were waited for; matrix products, arithmetic and copies ran while one was open for 5% of the time, Pallas kernels for 0%

profile of v1, /device:TPU:0, one launch (start us, length us, event | category | flops | bytes accessed | tf_op | source)
XLA Modules:
  0.0 338.3 jit_solution(10714621083495821996)
XLA Ops:
  7.2 0.7 all-gather.4.cloned.1.call-update
  8.0 3.1 collective-permute-start
  11.0 2.1 collective-permute-start.1
  13.1 53.0 %all_gather.12 = s32[512,8]{0,1:T(8,128)S(1)} all-gather(s32[128,8]{0,1:T(8,128)} %param.7), channel_id=1, replica_groups=mesh['blk'=8,'slab'=4] {'slab'}, dimensions={0}, use_global_device_ids=true | all-gather | bytes 20480 | tf_op jit(solution)/shard_map/all_gather | solution.py:42
  66.8 2.0 copy-done.2
  69.6 1.1 constant_dynamic-update-slice_fusion.2
  70.7 2.3 constant_dynamic-update-slice_fusion.1
  73.0 20.0 %collective-permute-done.2 = bf16[128,4096]{1,0:T(8,128)(2,1)S(1)} collective-permute-done((bf16[128,4096]{1,0:T(8,128)(2,1)S(1)}, bf16[128,4096]{1,0:T(8,128)(2,1)S(1)}, u32[]{:S(2)}, u32[]{:S(2)}) %collective-permute-start.2) | collective-permute-done | bytes 1048608 | tf_op jit(solution)/shard_map/ppermute | solution.py:33
  93.0 1.1 constant_dynamic-update-slice_fusion
  94.2 6.5 %convolution_multiply_fusion = f32[512,704]{0,1:T(8,128)S(1)} fusion(bf16[512,4096]{1,0:T(8,128)(2,1)} %constant_dynamic-update-slice_fusion, bf16[704,4096]{1,0:T(8,128)(2,1)} %all-gather.4.cloned.1.call-done), kind=kOutput, calls=%fused_computation.7 | convolution fusion | flops 2953150464 | bytes 11403264 | tf_op jit(solution)/shard_map/dot_general | solution.py:45
  100.8 33.0 %gather_fusion = f32[4096]{0:T(1024)S(1)} fusion(f32[512,704]{0,1:T(8,128)S(1)} %convolution_multiply_fusion, s32[4096]{0:T(1024)S(1)} %reshape.83), kind=kCustom, calls=%fused_computation | custom fusion | bytes 65536 | tf_op jit(solution)/shard_map/jit(take_along_axis)/gather | solution.py:54
  134.6 13.2 %all-gather.1 = f32[4,1,4352]{2,1,0:T(1,128)S(1)} all-gather(f32[1,1,4352]{2,1,0:T(1,128)S(1)} %reshape.105), channel_id=2, replica_groups=mesh['blk'=8,'slab'=4] {'slab'}, dimensions={0}, use_global_device_ids=true | all-gather | bytes 87040 | tf_op jit(solution)/shard_map/all_gather | solution.py:58
  147.8 0.6 reshape.81
  148.4 33.1 %gather_fusion.1 = f32[4096]{0:T(1024)S(1)} fusion(f32[4,512,8]{2,1,0:T(8,128)S(1)} %reshape.81, s32[4096]{0:T(1024)S(1)} %reshape.91), kind=kCustom, calls=%fused_computation.1 | custom fusion | bytes 81920 | tf_op jit(solution)/shard_map/jit(take_along_axis)/gather | solution.py:60
  181.9 1.5 select_reduce_fusion
  183.4 7.6 %convolution_convert_fusion = bf16[512,4096]{1,0:T(8,128)(2,1)} fusion(bf16[704,4096]{1,0:T(8,128)(2,1)} %all-gather.4.cloned.1.call-done, bf16[512,704]{0,1:T(8,128)(2,1)S(1)} %select_reduce_fusion), kind=kOutput, calls=%fused_computation.5 | convolution fusion | flops 2954887168 | bytes 10682368 | tf_op jit(solution)/shard_map/dot_general | solution.py:90
  191.3 0.6 fusion.17
  192.3 1.7 fusion.16
  193.9 0.5 copy-done.3
  194.4 5.0 %add_convert_fusion = bf16[704,4096]{1,0:T(8,128)(2,1)} fusion(f32[704,4096]{1,0:T(8,128)S(1)} %fusion.16, bf16[512,4096]{1,0:T(8,128)(2,1)S(1)} %copy-done.3, bf16[512,704]{0,1:T(8,128)(2,1)S(1)} %select_reduce_fusion), kind=kOutput, calls=%fused_computation.2 | convolution fusion | flops 2958557184 | bytes 22216704 | tf_op jit(solution)/shard_map/dot_general | solution.py:96
  199.5 66.5 %reduce-scatter.3.cloned.1.call-done = bf16[128,4096]{1,0:T(8,128)(2,1)} async-done(((bf16[512,4096]{1,0:T(8,128)(2,1)}), bf16[128,4096]{1,0:T(8,128)(2,1)}) %reduce-scatter.3.cloned.1.call-update) | async-done | bytes 1048592 | tf_op jit(solution)/shard_map/reduce_scatter | solution.py:91
  266.0 5.3 %convolution_add_fusion = f32[128,4096]{1,0:T(8,128)} fusion(bf16[704,4096]{1,0:T(8,128)(2,1)} %all-gather.4.cloned.1.call-done, bf16[128,4096]{1,0:T(8,128)(2,1)} %reduce-scatter.3.cloned.1.call-done, f32[512,704]{0,1:T(8,128)S(1)} %convolution_multiply_fusion, s32[]{:T(128)S(6)} %select_n.84, f32[128]{0:T(128)S(1)} %get-tuple-element.6, s32[128]{0:T(128)S(1)} %copy-done.4), kind=kOutput, calls=%fused_computation.6 | convolution fusion | flops 739696640 | bytes 9274372 | tf_op jit(solution)/shard_map/dot_general | solution.py:92
  271.3 58.1 %reduce-scatter.5.cloned.1.call-done = bf16[88,4096]{1,0:T(8,128)(2,1)} async-done(((bf16[704,4096]{1,0:T(8,128)(2,1)}), bf16[88,4096]{1,0:T(8,128)(2,1)}) %reduce-scatter.5.cloned.1.call-update) | async-done | bytes 720912 | tf_op jit(solution)/shard_map/reduce_scatter | solution.py:99
  329.4 2.3 convert_element_type.35
  (50 shorter events, 3.2 us)
Async XLA Ops:
  7.2 59.5 %copy-start = (bf16[128,4096]{1,0:T(8,128)(2,1)S(1)}, bf16[128,4096]{1,0:T(8,128)(2,1)}, u32[]{:S(2)}) copy-start(bf16[128,4096]{1,0:T(8,128)(2,1)} %param.4) | copy-start | bytes 3145732
  7.2 87.0 %all-gather.4.cloned.1.call-start = ((), (), s32[]{:S(2)}) async-start(), calls=%async_computation.2 | async-start | bytes 6488064 | tf_op jit(solution)/shard_map/all_gather | solution.py:17
  7.9 258.1 %reduce-scatter.3.cloned.1.call-start = ((), (), s32[]{:S(2)}) async-start(), calls=%async_computation.3 | async-start | bytes 5242880 | tf_op jit(solution)/shard_map/reduce_scatter | solution.py:91
  8.0 60.9 %collective-permute-start = (bf16[128,4096]{1,0:T(8,128)(2,1)}, bf16[128,4096]{1,0:T(8,128)(2,1)S(1)}, u32[]{:S(2)}, u32[]{:S(2)}) collective-permute-start(bf16[128,4096]{1,0:T(8,128)(2,1)} %param.4), channel_id=1, source_target_pairs={{0,1},{1,2},{2,3},{3,0},{4,5},{5,6},{6,7},{7,4},{8,9},{9,10},{10,1... | collective-permute-start | bytes 3145736 | tf_op jit(solution)/shard_map/ppermute | solution.py:33
  11.0 59.7 %collective-permute-start.1 = (bf16[128,4096]{1,0:T(8,128)(2,1)}, bf16[128,4096]{1,0:T(8,128)(2,1)}, u32[]{:S(2)}, u32[]{:S(2)}) collective-permute-start(bf16[128,4096]{1,0:T(8,128)(2,1)} %param.4), channel_id=1, source_target_pairs={{0,3},{1,0},{2,1},{3,2},{4,7},{5,4},{6,5},{7,6},{8,11},{9,8},{10,9... | collective-permute-start | bytes 3145736 | tf_op jit(solution)/shard_map/ppermute | solution.py:38
  66.7 2.0 copy-start.2
  68.9 24.2 %collective-permute-start.2 = (bf16[128,4096]{1,0:T(8,128)(2,1)S(1)}, bf16[128,4096]{1,0:T(8,128)(2,1)S(1)}, u32[]{:S(2)}, u32[]{:S(2)}) collective-permute-start(bf16[128,4096]{1,0:T(8,128)(2,1)S(1)} %collective-permute-done), channel_id=1, source_target_pairs={{0,1},{1,2},{2,3},{3,0},{4,5},{5,6},{6,7},{7,4},{8,9},{9,10},{10,1... | collective-permute-start | bytes 3145736 | tf_op jit(solution)/shard_map/ppermute | solution.py:33
  100.8 33.6 %copy-start.4 = (s32[128]{0:T(128)S(1)}, s32[128]{0:T(128)}, u32[]{:S(2)}) copy-start(s32[128]{0:T(128)} %param.6) | copy-start | bytes 1540
  191.0 1.2 copy-start.1
  191.1 138.3 %reduce-scatter.5.cloned.1.call-start = ((), (), s32[]{:S(2)}) async-start(), calls=%async_computation.4 | async-start | bytes 6488064 | tf_op jit(solution)/shard_map/reduce_scatter | solution.py:99
  192.3 2.2 copy-start.3
Sparse Core Ops, SparseCore 0:
  9.9 46.0 all-gather.3
  191.2 74.7 reduce-scatter.2
  269.8 59.5 reduce-scatter.4
